TPU v7x, 32 devices: a whole 2x2x4 slice. The times are simulated.
32 devices in a mesh: ctx: 8 (over y, x, core), mp: 4 (over z).
Axes of the slice: x: 2, y: 2, z: 4, core: 2. Of those that a mesh axis runs over, the one named last changes fastest.
Arguments:
- cotangent: bfloat16 [1536, 8192], P('ctx', 'mp'), may hold values from -6 to 6
- out_weight: bfloat16 [8192, 8192], P('mp', 'ctx'), may hold values from -0.0625 to 0.0625
- query_act: bfloat16 [1536, 8192], P('ctx', 'mp'), may hold values from -6 to 6
- key_act: bfloat16 [1536, 8192], P('ctx', 'mp'), may hold values from -6 to 6
- value_act: bfloat16 [1536, 8192], P('ctx', 'mp'), may hold values from -6 to 6
- filters: float32 [512, 128], replicated, may hold values from -0.5 to 0.5
Outputs:
- grad_query: bfloat16 [1536, 8192], P('ctx', 'mp')
- grad_key: bfloat16 [1536, 8192], P('ctx', 'mp')
- grad_value: bfloat16 [1536, 8192], P('ctx', 'mp')
- grad_filters: float32 [512, 128], replicated
All inputs are finite; a program needn't handle non-finite values.
Results may differ from a plain program's by a relative error of at most 0.0051.
Values may be sent and summed in bfloat16 or wider, within the bound.
No kernel may reach another device: no remote copies, remote signals or barrier semaphores. Data moves between devices by JAX's collectives and lax.ppermute only.
A program may use at most 128 MiB of HBM per device.

v0:
```python
import jax
import jax.numpy as jnp
from jax import lax
from jax.sharding import PartitionSpec as P


def causal(widened, taps, rows, prev):

    def causal_step(shift, total):
        window = lax.dynamic_slice_in_dim(widened, (prev - shift).astype(jnp.int32), rows, 0)
        weight = lax.dynamic_slice_in_dim(taps, shift.astype(jnp.int32), 1, 0)
        return total + weight * window

    return lax.fori_loop(
        jnp.int32(0),
        jnp.int32(prev + 1),
        causal_step,
        jnp.zeros((rows, widened.shape[1]), widened.dtype),
    )


def anticausal(trailing, taps, rows, prev):

    def anticausal_step(shift, total):
        window = lax.dynamic_slice_in_dim(trailing, shift.astype(jnp.int32), rows, 0)
        weight = lax.dynamic_slice_in_dim(taps, shift.astype(jnp.int32), 1, 0)
        return total + weight * window

    return lax.fori_loop(
        jnp.int32(0),
        jnp.int32(prev + 1),
        anticausal_step,
        jnp.zeros((rows, trailing.shape[1]), trailing.dtype),
    )


def lagged(widened, gradient, prev):
    rows = gradient.shape[0]

    def one_lag(shift):
        window = lax.dynamic_slice_in_dim(widened, prev - shift, rows, 0)
        return jnp.sum(window * gradient, axis=0)

    return lax.map(one_lag, jnp.arange(prev + 1, dtype=jnp.int32))


def contract(left, right):
    return lax.dot_general(
        left, right, (((1,), (1,)), ((), ())), preferred_element_type=jnp.float32
    )


def group_table(first, count, per_group, groups):
    channel = first + jnp.arange(count)
    return (channel[None, :] // per_group == jnp.arange(groups)[:, None]).astype(jnp.float32)


def body(cotangent, out_weight, query_act, key_act, value_act, filters):
    tok_rows, chans = cotangent.shape
    groups, taps_len = filters.shape
    prev = taps_len - 1
    ctx_count = lax.axis_size("ctx")
    per_group = chans * lax.axis_size("mp") // groups
    panel = lax.all_gather(out_weight, "ctx", axis=1, tiled=True)
    grad_mixed = contract(lax.all_gather(cotangent, "mp", axis=1, tiled=True), panel)
    product = (key_act.astype(jnp.float32) * value_act.astype(jnp.float32)).astype(jnp.bfloat16)
    grad_conv = (grad_mixed * query_act.astype(jnp.float32)).astype(jnp.bfloat16)
    narrow = chans // ctx_count
    seq_product, seq_grad = (
        lax.all_to_all(product, "ctx", split_axis=1, concat_axis=0, tiled=True),
        lax.all_to_all(grad_conv, "ctx", split_axis=1, concat_axis=0, tiled=True),
    )
    onehot = group_table(
        lax.axis_index("mp") * chans + lax.axis_index("ctx") * narrow, narrow, per_group, groups
    )
    taps = jnp.dot(filters.T, onehot, precision=lax.Precision.HIGHEST)
    seq_rows = seq_grad.shape[0]
    grad_wide = seq_grad.astype(jnp.float32)
    widened = jnp.concatenate(
        [jnp.zeros((prev, narrow), jnp.float32), seq_product.astype(jnp.float32)], 0
    )
    trailing = jnp.concatenate([grad_wide, jnp.zeros((prev, narrow), jnp.float32)], 0)
    seq_mixed = causal(widened, taps, seq_rows, prev)
    seq_back = anticausal(trailing, taps, seq_rows, prev)
    corr = lagged(widened, grad_wide, prev)
    mixed, grad_product = (
        lax.all_to_all(seq_mixed, "ctx", split_axis=0, concat_axis=1, tiled=True),
        lax.all_to_all(seq_back, "ctx", split_axis=0, concat_axis=1, tiled=True),
    )
    grad_query = (grad_mixed * mixed).astype(jnp.bfloat16)
    grad_key = (grad_product * value_act.astype(jnp.float32)).astype(jnp.bfloat16)
    grad_value = (grad_product * key_act.astype(jnp.float32)).astype(jnp.bfloat16)
    partial_terms = jnp.dot(onehot, corr.T, precision=lax.Precision.HIGHEST)
    scale = (tok_rows * ctx_count * per_group) ** (-0.5)
    grad_filters = lax.psum(partial_terms, ("ctx", "mp")) * scale
    return (grad_query, grad_key, grad_value, grad_filters)


def solution(mesh):
    in_specs = (P("ctx", "mp"), P("mp", "ctx"), P("ctx", "mp"), P("ctx", "mp"), P("ctx", "mp"), P())
    out_specs = (P("ctx", "mp"), P("ctx", "mp"), P("ctx", "mp"), P())
    return jax.shard_map(body, mesh=mesh, in_specs=in_specs, out_specs=out_specs, check_vma=False)
```

profile of v0, /device:TPU:0, one launch (start us, length us, event | category | flops | bytes accessed | tf_op | source)
XLA Modules:
  0.0 1397.0 jit_solution(9679557478164837878)
XLA Ops:
  8.7 67.1 %all-gather.3.cloned.1.call-done = bf16[192,8192]{1,0:T(8,128)(2,1)} async-done(((bf16[192,2048]{1,0:T(8,128)(2,1)}), bf16[192,8192]{1,0:T(8,128)(2,1)}) %all-gather.3.cloned.1.call-update) | async-done | bytes 3145744 | tf_op jit(solution)/shard_map/all_gather | solution.py:65
  75.8 161.4 %all-gather.5.cloned.1.call-done = bf16[2048,8192]{1,0:T(8,128)(2,1)} async-done(((bf16[2048,1024]{1,0:T(8,128)(2,1)}), bf16[2048,8192]{1,0:T(8,128)(2,1)}) %all-gather.5.cloned.1.call-update) | async-done | bytes 33554448 | tf_op jit(solution)/shard_map/all_gather | solution.py:64
  237.2 18.0 %multiply_convert_fusion = (bf16[192,2048]{1,0:T(8,128)(2,1)S(1)}, f32[192,2048]{1,0:T(8,128)}) fusion(bf16[192,2048]{1,0:T(8,128)(2,1)S(1)} %copy-done.7, bf16[192,8192]{1,0:T(8,128)(2,1)} %all-gather.3.cloned.1.call-done, bf16[2048,8192]{1,0:T(8,128)(2,1)} %all-gather.5.cloned.1.call-done), kind=kOutput, calls=%fused_computation.11 | convolution fusion | flops 6443630592 | bytes 39845888 | tf_op jit(solution)/shard_map/dot_general | solution.py:48
  256.1 3.5 all-to-all-start.2
  260.5 11.8 all-to-all-done.2
  274.4 282.6 %while.38 = (s32[]{:T(128)}, f32[1536,256]{1,0:T(8,128)S(1)}, f32[128,256]{1,0:T(8,128)S(1)}, f32[1663,256]{1,0:T(8,128)}, s32[]{:T(128)}, /*index=5*/s32[]{:T(128)}) while((s32[]{:T(128)}, f32[1536,256]{1,0:T(8,128)S(1)}, f32[128,256]{1,0:T(8,128)S(1)}, f32[1663,256]{1,0:T(8,128)}, s32[]{:T(128)}, /*index=5*/s32[]{:T(128)}) %tuple.98), condition=%wide.region_3.4_spmd.clone, body=%wide.region_2.3_spmd.clone.sunk | while | flops 1179651 | bytes 4721759 | solution.py:29
  557.0 23.4 %all_to_all.64 = f32[8,192,256]{2,1,0:T(8,128)S(1)} all-to-all(f32[8,192,256]{2,1,0:T(8,128)S(1)} %bitcast.45), channel_id=1, replica_groups=mesh['ctx'=8,'mp'=4] {'ctx'}, dimensions={0} | all-to-all | bytes 3145728 | tf_op jit(solution)/shard_map/all_to_all | solution.py:88
  584.3 3.5 all-to-all-start
  587.9 12.5 all-to-all-done
  602.6 364.1 %while.37 = (s32[]{:T(128)}, f32[1536,256]{1,0:T(8,128)}, f32[128,256]{1,0:T(8,128)S(1)}, f32[1663,256]{1,0:T(8,128)S(1)}, s32[]{:T(128)}, /*index=5*/s32[]{:T(128)}, s32[]{:T(128)}, s32[]{:T(128)}) while((s32[]{:T(128)}, f32[1536,256]{1,0:T(8,128)}, f32[128,256]{1,0:T(8,128)S(1)}, f32[1663,256]{1,0:T(8,128)S(1)}, s32[]{:T(128)}, ...), condition=%wide.region_1.2_spmd.clone, body=%wide.region_0.1_spmd.clone.sunk | while | flops 1179655 | bytes 4721821 | solution.py:14
  607.0 2.9 select_add_fusion.4
  609.9 2.9 select_add_fusion.4
  618.6 2.9 select_add_fusion.4
  621.5 2.9 select_add_fusion.4
  646.9 2.9 select_add_fusion.4
  652.7 2.9 select_add_fusion.4
  655.6 2.9 select_add_fusion.4
  664.3 2.9 select_add_fusion.4
  667.2 2.9 select_add_fusion.4
  692.6 2.9 select_add_fusion.4
  698.4 2.9 select_add_fusion.4
  701.3 2.9 select_add_fusion.4
  710.0 2.9 select_add_fusion.4
  712.9 2.9 select_add_fusion.4
  738.3 2.9 select_add_fusion.4
  744.1 2.9 select_add_fusion.4
  747.0 2.9 select_add_fusion.4
  755.6 2.9 select_add_fusion.4
  758.5 2.9 select_add_fusion.4
  966.7 4.3 all-to-all-start.1
  971.0 287.3 %while.36 = (s32[]{:T(128)}, f32[128,256]{1,0:T(8,128)S(1)}, s32[128]{0:T(128)S(1)}, f32[1663,256]{1,0:T(8,128)S(1)}, f32[1536,256]{1,0:T(8,128)S(1)}, /*index=5*/s32[]{:T(128)}, s32[1]{0:T(128)}, s32[]{:T(128)}, s32[1]{0:T(128)}) while((s32[]{:T(128)}, f32[128,256]{1,0:T(8,128)S(1)}, s32[128]{0:T(128)S(1)}, f32[1663,256]{1,0:T(8,128)S(1)}, ...), condition=%wide.region_6.7_spmd, body=%wide.region_4.6_spmd.sunk | while | flops 786182 | bytes 3148967 | solution.py:44
  1259.5 126.4 %all-reduce.4.cloned.1.call-done = f32[512,128]{1,0:T(8,128)} async-done(((f32[512,128]{1,0:T(8,128)}), f32[512,128]{1,0:T(8,128)}) %all-reduce.4.cloned.1.call-update) | async-done | bytes 262160 | tf_op jit(solution)/shard_map/psum | solution.py:95
  (918 shorter events, 722.9 us)
Async XLA Ops:
  7.2 252.6 %copy-start = (f32[512,128]{1,0:T(8,128)S(1)}, f32[512,128]{1,0:T(8,128)}, u32[]{:S(2)}) copy-start(f32[512,128]{1,0:T(8,128)} %param.17) | copy-start | bytes 786436
  7.2 68.6 %all-gather.3.cloned.1.call-start = ((), (), s32[]{:S(2)}) async-start(), calls=%async_computation.4 | async-start | bytes 3932160 | tf_op jit(solution)/shard_map/all_gather | solution.py:65
  7.9 229.3 %copy-start.7 = (bf16[192,2048]{1,0:T(8,128)(2,1)S(1)}, bf16[192,2048]{1,0:T(8,128)(2,1)}, u32[]{:S(2)}) copy-start(bf16[192,2048]{1,0:T(8,128)(2,1)} %param.14) | copy-start | bytes 2359300
  7.9 229.3 %all-gather.5.cloned.1.call-start = ((), (), s32[]{:S(2)}) async-start(), calls=%async_computation.5 | async-start | bytes 37748736 | tf_op jit(solution)/shard_map/all_gather | solution.py:64
  256.1 16.1 %all-to-all-start.2 = ((bf16[192,8,256]{2,0,1:T(8,128)(2,1)}), bf16[192,8,256]{2,0,1:T(8,128)(2,1)S(1)}, u32[]{:S(2)}, u32[]{:S(2)}) async-start(bf16[192,8,256]{2,0,1:T(8,128)(2,1)} %bitcast.31), calls=%async_computation.2 | async-start | bytes 1572864 | tf_op jit(solution)/shard_map/all_to_all | solution.py:71
  272.4 2.0 copy-start.2
  580.4 1.1 copy-start.5
  580.4 1.4 copy-start.6
  584.3 16.1 %all-to-all-start = ((bf16[192,8,256]{2,0,1:T(8,128)(2,1)}), bf16[192,8,256]{2,0,1:T(8,128)(2,1)S(1)}, u32[]{:S(2)}, u32[]{:S(2)}) async-start(bf16[192,8,256]{2,0,1:T(8,128)(2,1)} %bitcast.32), calls=%async_computation | async-start | bytes 1572864 | tf_op jit(solution)/shard_map/all_to_all | solution.py:70
  600.4 0.9 copy-start.3
  966.7 420.9 %all-to-all-start.1 = ((f32[8,192,256]{2,1,0:T(8,128)}), f32[8,192,256]{2,1,0:T(8,128)}, u32[]{:S(2)}, u32[]{:S(2)}) async-start(f32[8,192,256]{2,1,0:T(8,128)} %bitcast.46), calls=%async_computation.1 | async-start | bytes 3145728 | tf_op jit(solution)/shard_map/all_to_all | solution.py:87
  970.9 414.9 %all-reduce.4.cloned.1.call-start = ((), (), s32[]{:S(2)}) async-start(), calls=%async_computation.6 | async-start | bytes 524288 | tf_op jit(solution)/shard_map/psum | solution.py:95
  1387.5 1.9 copy-start.4
  1389.2 1.3 copy-start.1
Sparse Core Ops, SparseCore 0:
  9.6 66.1 all-gather.2
  77.7 159.4 all-gather.4
  1259.6 126.2 all-reduce.3
where the time goes:
time: 1410 us; the launch traced here: 1400 us
  other arithmetic  685 us (49%)
  waiting for transfers between devices  381 us (27%)
  loops' own time  173 us (12%)
  local copies, waits for them, and re-layouts  89.3 us (6%)
  blocking collectives  23.4 us (2%)
  matrix products  19.7 us (1%)
    add x128, other arithmetic, causal_step(): return total + weight * window  363 us
    add x128, other arithmetic, anticausal_step(): return total + weight * window  278 us
    another operation x1, loops' own time, lagged(): return lax.map(one_lag, jnp.arange(prev + 1, dtype=jnp.int32))  169 us
    all_gather x1, waiting for transfers between devices, body(): panel = lax.all_gather(out_weight, 'ctx', axis=1, tiled=True)  161 us
    psum x1, waiting for transfers between devices, body(): grad_filters = lax.psum(partial_terms, ('ctx', 'mp')) * scale  126 us
    dynamic_slice x128, local copies, waits for them, and re-layouts, lagged(): return lax.map(one_lag, jnp.arange(prev + 1, dtype=jnp.int32))  75 us
    all_gather x1, waiting for transfers between devices, body(): lax.all_gather(cotangent, 'mp', axis=1, tiled=True)  67.1 us
    reduce_sum x128, other arithmetic, one_lag(): return jnp.sum(window * gradient, axis=0)  38.9 us
  transfers between devices with their start and end apart: 6, of which 5 were waited for; matrix products, arithmetic and copies ran while one was open for 9% of the time, Pallas kernels for 0%

commit v1 on v0

--- a/solution.py
+++ b/solution.py
@@ -92,7 +92,7 @@
     grad_value = (grad_product * key_act.astype(jnp.float32)).astype(jnp.bfloat16)
     partial_terms = jnp.dot(onehot, corr.T, precision=lax.Precision.HIGHEST)
     scale = (tok_rows * ctx_count * per_group) ** (-0.5)
-    grad_filters = lax.psum(partial_terms, ("ctx", "mp")) * scale
+    grad_filters = jnp.sum(lax.all_gather(partial_terms, ("ctx", "mp")), axis=0) * scale
     return (grad_query, grad_key, grad_value, grad_filters)
 
 

time: 1410 us -> 1320 us (0.936)
  waiting for transfers between devices: 381 us -> 254 us
  blocking collectives: 23.4 us -> 47.9 us
  other arithmetic: 685 us -> 701 us
    psum x1 -> x0, waiting for transfers between devices: 126 us -> none  [body(): grad_filters = lax.psum(partial_terms, ('ctx', 'mp')) * scale]
    all_to_all x0 -> x1, blocking collectives: none -> 24.5 us  [body(): lax.all_to_all(seq_mixed, 'ctx', split_axis=0, concat_axis=1, tiled=True)]
  transfers between devices with their start and end apart: 6 -> 5, of which waited for: 5 -> 4; matrix products, arithmetic and copies ran while one was open for 9% -> 29% of each run, Pallas kernels for 0% -> 0%
where the time goes in v1:
time: 1320 us; the launch traced here: 1310 us
  other arithmetic  701 us (53%)
  waiting for transfers between devices  254 us (19%)
  loops' own time  173 us (13%)
  local copies, waits for them, and re-layouts  88.1 us (7%)
  blocking collectives  47.9 us (4%)
  matrix products  19.7 us (1%)
  between operations  13.9 us (1%)
    add x128, other arithmetic, causal_step(): return total + weight * window  375 us
    add x128, other arithmetic, anticausal_step(): return total + weight * window  278 us
    another operation x1, loops' own time, lagged(): return lax.map(one_lag, jnp.arange(prev + 1, dtype=jnp.int32))  169 us
    all_gather x1, waiting for transfers between devices, body(): panel = lax.all_gather(out_weight, 'ctx', axis=1, tiled=True)  161 us
    dynamic_slice x128, local copies, waits for them, and re-layouts, lagged(): return lax.map(one_lag, jnp.arange(prev + 1, dtype=jnp.int32))  75 us
    all_gather x1, waiting for transfers between devices, body(): lax.all_gather(cotangent, 'mp', axis=1, tiled=True)  67.1 us
    reduce_sum x128, other arithmetic, one_lag(): return jnp.sum(window * gradient, axis=0)  38.9 us
  transfers between devices with their start and end apart: 5, of which 4 were waited for; matrix products, arithmetic and copies ran while one was open for 29% of the time, Pallas kernels for 0%

profile of v1, /device:TPU:0, one launch (start us, length us, event | category | flops | bytes accessed | tf_op | source)
XLA Modules:
  0.0 1305.7 jit_solution(8903504853123754538)
XLA Ops:
  8.7 67.1 %all-gather.5.cloned.1.call-done = bf16[192,8192]{1,0:T(8,128)(2,1)} async-done(((bf16[192,2048]{1,0:T(8,128)(2,1)}), bf16[192,8192]{1,0:T(8,128)(2,1)}) %all-gather.5.cloned.1.call-update) | async-done | bytes 3145744 | tf_op jit(solution)/shard_map/all_gather | solution.py:65
  75.8 161.4 %all-gather.7.cloned.1.call-done = bf16[2048,8192]{1,0:T(8,128)(2,1)} async-done(((bf16[2048,1024]{1,0:T(8,128)(2,1)}), bf16[2048,8192]{1,0:T(8,128)(2,1)}) %all-gather.7.cloned.1.call-update) | async-done | bytes 33554448 | tf_op jit(solution)/shard_map/all_gather | solution.py:64
  237.2 18.0 %multiply_convert_fusion = (bf16[192,2048]{1,0:T(8,128)(2,1)S(1)}, f32[192,2048]{1,0:T(8,128)}) fusion(bf16[192,2048]{1,0:T(8,128)(2,1)S(1)} %copy-done.6, bf16[192,8192]{1,0:T(8,128)(2,1)} %all-gather.5.cloned.1.call-done, bf16[2048,8192]{1,0:T(8,128)(2,1)} %all-gather.7.cloned.1.call-done), kind=kOutput, calls=%fused_computation.11 | convolution fusion | flops 6443630592 | bytes 39845888 | tf_op jit(solution)/shard_map/dot_general | solution.py:48
  256.1 4.2 all-to-all-start.2
  261.1 11.9 all-to-all-done.2
  275.6 282.6 %while.38 = (s32[]{:T(128)}, f32[1536,256]{1,0:T(8,128)S(1)}, f32[128,256]{1,0:T(8,128)S(1)}, f32[1663,256]{1,0:T(8,128)}, s32[]{:T(128)}, /*index=5*/s32[]{:T(128)}) while((s32[]{:T(128)}, f32[1536,256]{1,0:T(8,128)S(1)}, f32[128,256]{1,0:T(8,128)S(1)}, f32[1663,256]{1,0:T(8,128)}, s32[]{:T(128)}, /*index=5*/s32[]{:T(128)}) %tuple.81), condition=%wide.region_3.4_spmd.clone, body=%wide.region_2.3_spmd.clone.sunk | while | flops 1179651 | bytes 4721759 | solution.py:29
  558.1 23.4 %all_to_all.64 = f32[8,192,256]{2,1,0:T(8,128)S(1)} all-to-all(f32[8,192,256]{2,1,0:T(8,128)S(1)} %bitcast.47), channel_id=1, replica_groups=mesh['ctx'=8,'mp'=4] {'ctx'}, dimensions={0} | all-to-all | bytes 3145728 | tf_op jit(solution)/shard_map/all_to_all | solution.py:88
  585.5 3.5 all-to-all-start
  589.1 12.5 all-to-all-done
  603.8 287.3 %while.36 = (s32[]{:T(128)}, f32[128,256]{1,0:T(8,128)S(1)}, s32[128]{0:T(128)S(1)}, f32[1663,256]{1,0:T(8,128)S(1)}, f32[1536,256]{1,0:T(8,128)S(1)}, /*index=5*/s32[]{:T(128)}, s32[1]{0:T(128)}, s32[]{:T(128)}, s32[1]{0:T(128)}) while((s32[]{:T(128)}, f32[128,256]{1,0:T(8,128)S(1)}, s32[128]{0:T(128)S(1)}, f32[1663,256]{1,0:T(8,128)S(1)}, ...), condition=%wide.region_6.7_spmd, body=%wide.region_4.6_spmd.sunk | while | flops 786182 | bytes 3148967 | solution.py:44
  892.2 375.4 %while.37 = (s32[]{:T(128)}, f32[1536,256]{1,0:T(8,128)}, f32[128,256]{1,0:T(8,128)S(1)}, f32[1663,256]{1,0:T(8,128)S(1)}, s32[]{:T(128)}, /*index=5*/s32[]{:T(128)}, s32[]{:T(128)}, s32[]{:T(128)}) while((s32[]{:T(128)}, f32[1536,256]{1,0:T(8,128)}, f32[128,256]{1,0:T(8,128)S(1)}, f32[1663,256]{1,0:T(8,128)S(1)}, s32[]{:T(128)}, ...), condition=%wide.region_1.2_spmd.clone, body=%wide.region_0.1_spmd.clone.sunk | while | flops 1179655 | bytes 4721821 | solution.py:14
  896.8 3.0 select_add_fusion.4
  899.8 3.0 select_add_fusion.4
  905.8 3.0 select_add_fusion.4
  908.8 3.0 select_add_fusion.4
  937.9 3.2 select_add_fusion.4
  944.1 3.0 select_add_fusion.4
  950.1 3.0 select_add_fusion.4
  953.1 3.0 select_add_fusion.4
  956.1 3.0 select_add_fusion.4
  959.1 3.0 select_add_fusion.4
  965.0 3.0 select_add_fusion.4
  985.4 3.0 select_add_fusion.4
  991.4 3.0 select_add_fusion.4
  997.4 3.0 select_add_fusion.4
  1006.3 3.0 select_add_fusion.4
  1035.4 3.0 select_add_fusion.4
  1041.4 3.0 select_add_fusion.4
  1047.4 3.0 select_add_fusion.4
  1050.4 3.0 select_add_fusion.4
  1267.6 24.5 %all_to_all.65 = f32[8,192,256]{2,1,0:T(8,128)S(1)} all-to-all(f32[8,192,256]{2,1,0:T(8,128)} %bitcast.46), channel_id=1, replica_groups=mesh['ctx'=8,'mp'=4] {'ctx'}, dimensions={0} | all-to-all | bytes 3145728 | tf_op jit(solution)/shard_map/all_to_all | solution.py:87
  1294.6 3.8 reduce_sum.21
  (916 shorter events, 731.3 us)
Async XLA Ops:
  7.2 253.2 %copy-start = (f32[512,128]{1,0:T(8,128)S(1)}, f32[512,128]{1,0:T(8,128)}, u32[]{:S(2)}) copy-start(f32[512,128]{1,0:T(8,128)} %param.17) | copy-start | bytes 786436
  7.2 68.6 %all-gather.5.cloned.1.call-start = ((), (), s32[]{:S(2)}) async-start(), calls=%async_computation.4 | async-start | bytes 3932160 | tf_op jit(solution)/shard_map/all_gather | solution.py:65
  7.9 229.3 %copy-start.6 = (bf16[192,2048]{1,0:T(8,128)(2,1)S(1)}, bf16[192,2048]{1,0:T(8,128)(2,1)}, u32[]{:S(2)}) copy-start(bf16[192,2048]{1,0:T(8,128)(2,1)} %param.14) | copy-start | bytes 2359300
  7.9 229.3 %all-gather.7.cloned.1.call-start = ((), (), s32[]{:S(2)}) async-start(), calls=%async_computation.5 | async-start | bytes 37748736 | tf_op jit(solution)/shard_map/all_gather | solution.py:64
  256.1 16.8 %all-to-all-start.2 = ((bf16[192,8,256]{2,0,1:T(8,128)(2,1)}), bf16[192,8,256]{2,0,1:T(8,128)(2,1)}, u32[]{:S(2)}, u32[]{:S(2)}) async-start(bf16[192,8,256]{2,0,1:T(8,128)(2,1)} %bitcast.32), calls=%async_computation.2 | async-start | bytes 1572864 | tf_op jit(solution)/shard_map/all_to_all | solution.py:71
  581.6 1.1 copy-start.4
  581.6 1.4 copy-start.5
  585.5 16.1 %all-to-all-start = ((bf16[192,8,256]{2,0,1:T(8,128)(2,1)}), bf16[192,8,256]{2,0,1:T(8,128)(2,1)S(1)}, u32[]{:S(2)}, u32[]{:S(2)}) async-start(bf16[192,8,256]{2,0,1:T(8,128)(2,1)} %bitcast.33), calls=%async_computation | async-start | bytes 1572864 | tf_op jit(solution)/shard_map/all_to_all | solution.py:70
  589.0 705.5 %all-gather.9.cloned.1.call-start = ((), (), s32[]{:S(2)}) async-start(), calls=%async_computation.6 | async-start | bytes 8650752 | tf_op jit(solution)/shard_map/all_gather | solution.py:95
  601.6 0.9 copy-start.2
  1292.1 1.4 copy-start.3
  1294.6 4.6 copy-start.1
Sparse Core Ops, SparseCore 0:
  9.6 66.1 all-gather.4
  77.7 159.4 all-gather.6
  892.3 76.4 all-gather.8
